TPU v7x, 512 devices: a whole 4x8x8 slice. The times are simulated.
512 devices in a mesh: req: 64 (over z, x, core), voc: 8 (over y).
Axes of the slice: x: 4, y: 8, z: 8, core: 2. Of those that a mesh axis runs over, the one named last changes fastest.
Arguments:
- hidden: bfloat16 [65536, 1600], P(('req', 'voc')), may hold values from -60 to 60
- norm_gain: float32 [1600], replicated, may hold values from 0.25 to 1.75
- unembed: bfloat16 [16384, 1600], P(('req', 'voc')), may hold values from -2 to 2
- targets: int32 [65536], P(('req', 'voc')), may hold values from 0 to 16383
- live: int32 [65536], P(('req', 'voc')), may hold values from 0 to 1, as said below
Outputs:
- logprob: float32 [65536], P(('req', 'voc'))
- entropy: float32 [65536], P(('req', 'voc'))
Inputs may be any that keep to these rules, and one draw needn't show every extreme that they name: Within each aligned block of 1024 slots (one owner's) the live slots form a prefix of 128 to 1024 slots, and in every draw at least one block is wholly live.
All inputs are finite; a program needn't handle non-finite values.
Results may differ from a plain program's by a relative error of at most 0.0067.
Values may be sent and summed in bfloat16 or wider, within the bound.
No kernel may reach another device: no remote copies, remote signals or barrier semaphores. Data moves between devices by JAX's collectives and lax.ppermute only.
A program may use at most 64 MiB of HBM per device.

v0:
```python
import jax
import jax.numpy as jnp
from jax import lax
from jax.sharding import PartitionSpec as P


def merged_2(value, axis, join):
    pieces = jax.tree.map(lambda part: lax.all_gather(part, axis), value)
    head = jax.tree.map(lambda part: part[0], pieces)
    tail = jax.tree.map(lambda part: part[1:], pieces)
    so_far, _ = lax.scan(lambda so_far, piece: (join(so_far, piece), None), head, tail)
    return so_far


def combine_stats(first, second):
    top = jnp.maximum(first[0], second[0])
    scale_one = jnp.exp(first[0] - top)
    scale_two = jnp.exp(second[0] - top)
    total = first[1] * scale_one + second[1] * scale_two
    spread = scale_one * (first[2] + (first[0] - top) * first[1]) + scale_two * (
        second[2] + (second[0] - top) * second[1]
    )
    return (top, total, spread, first[3] + second[3])


def on_device(hidden, norm_gain, unembed, targets, live):
    rows, wanted = (
        lax.all_gather(hidden, "voc", axis=0, tiled=True),
        lax.all_gather(targets, "voc", axis=0, tiled=True),
    )
    wide = rows.astype(jnp.float32)
    normed = (
        wide * lax.rsqrt(jnp.mean(wide * wide, axis=1, keepdims=True) + 1e-06) * norm_gain
    ).astype(jnp.bfloat16)
    groups = lax.axis_size("voc")
    column = lax.axis_index("voc")
    width = unembed.shape[0]
    count = normed.shape[0]
    zeros = jnp.zeros((count,), jnp.float32)
    start_carry = (jnp.full((count,), -1e30, jnp.float32), zeros, zeros, zeros)
    whole = lax.all_gather(unembed, "req", axis=0, tiled=True)
    stats = start_carry
    step = min(512, whole.shape[0])
    for first in range(0, whole.shape[0], step):
        piece = whole[first : first + step]
        logits = lax.dot_general(
            normed, piece, (((1,), (1,)), ((), ())), preferred_element_type=jnp.float32
        )
        local = first + jnp.arange(piece.shape[0], dtype=jnp.int32)
        vocab_ids = local // width * (groups * width) + column * width + local % width
        chosen = jnp.sum(jnp.where(vocab_ids[None, :] == wanted[:, None], logits, 0.0), axis=1)
        fold_top = jnp.max(logits, axis=1)
        shifted = logits - fold_top[:, None]
        weights = jnp.exp(shifted)
        newer = (fold_top, jnp.sum(weights, axis=1), jnp.sum(weights * shifted, axis=1), chosen)
        stats = combine_stats(stats, newer)
    mine = count // groups
    merged = merged_2(stats, "voc", combine_stats)
    top = lax.dynamic_slice_in_dim(merged[0], column * mine, mine)
    total = lax.dynamic_slice_in_dim(merged[1], column * mine, mine)
    spread = lax.dynamic_slice_in_dim(merged[2], column * mine, mine)
    picked = lax.dynamic_slice_in_dim(merged[3], column * mine, mine)
    mask = live.astype(jnp.float32)
    logprob = (picked - top - jnp.log(total)) * mask
    entropy = (jnp.log(total) - spread / total) * mask
    return (logprob, entropy)


def solution(mesh):
    return jax.shard_map(
        on_device,
        mesh=mesh,
        in_specs=(
            P(("req", "voc"), None),
            P(),
            P(("req", "voc"), None),
            P(("req", "voc")),
            P(("req", "voc")),
        ),
        out_specs=(P(("req", "voc")), P(("req", "voc"))),
        check_vma=False,
    )
```

profile of v0, /device:TPU:16, one launch (start us, length us, event | category | flops | bytes accessed | tf_op | source)
XLA Modules:
  0.0 284.1 jit_solution(10954525450019727820)
XLA Ops:
  7.2 0.0 copy-start.3
  7.2 0.0 all-gather.8.cloned.1.call-start
  7.2 0.7 all-gather.8.cloned.1.call-update
  7.9 0.0 all-gather.10.cloned.1.call-start
  8.0 0.7 all-gather.10.cloned.1.call-update
  8.7 16.5 %all-gather.4 = s32[8,1,128]{2,1,0:T(1,128)S(1)} all-gather(s32[1,1,128]{2,1,0:T(1,128)} %bitcast.74), channel_id=1, replica_groups=mesh['req'=64,'voc'=8] {'voc'}, dimensions={0}, use_global_device_ids=true | all-gather | bytes 4608 | tf_op jit(solution)/shard_map/all_gather | solution.py:29
  25.1 46.9 %all-gather.8.cloned.1.call-done = bf16[1024,1600]{0,1:T(8,128)(2,1)} async-done(((bf16[128,1600]{0,1:T(8,128)(2,1)}), bf16[1024,1600]{0,1:T(8,128)(2,1)}) %all-gather.8.cloned.1.call-update) | async-done | bytes 3276816 | tf_op jit(solution)/shard_map/all_gather | solution.py:28
  72.1 0.0 copy-start
  72.1 2.8 fusion
  74.9 87.4 %all-gather.10.cloned.1.call-done = bf16[2048,1600]{1,0:T(8,128)(2,1)} async-done(((bf16[32,1600]{1,0:T(8,128)(2,1)}), bf16[2048,1600]{1,0:T(8,128)(2,1)}) %all-gather.10.cloned.1.call-update) | async-done | bytes 6553616 | tf_op jit(solution)/shard_map/all_gather | solution.py:41
  162.3 0.0 copy-done.3
  162.3 0.0 copy-done
  162.3 0.0 copy-start.2
  162.3 3.8 %fusion.44 = (f32[1024]{0:T(1024)S(1)}, f32[1024,512]{0,1:T(8,128)S(1)}) fusion(bf16[1024,1600]{0,1:T(8,128)(2,1)S(1)} %copy-done, f32[1600]{0:T(1024)S(1)} %copy-done.3, f32[1024]{0:T(1024)S(1)} %add_rsqrt_fusion, bf16[2048,1600]{1,0:T(8,128)(2,1)} %all-gather.10.cloned.1.call-done), kind=kOutput, calls=%fused_computation.103 | convolution fusion | flops 1684798464 | bytes 7092480 | tf_op jit(solution)/shard_map/dot_general | solution.py:46
  166.2 0.0 copy-done.2
  166.2 2.2 fusion.45
  168.4 2.2 fusion.46
  170.7 2.2 fusion.47
  172.9 0.0 copy-start.1
  173.0 3.9 %fusion.3 = (f32[1024]{0:T(1024)S(1)}, f32[1024]{0:T(1024)S(1)}, f32[1024]{0:T(1024)S(1)}, f32[1024]{0:T(1024)S(1)}, f32[1024]{0:T(1024)S(1)}, /*index=5*/f32[10...) fusion(f32[1024,512]{0,1:T(8,128)S(1)} %get-tuple-element.108, ...), kind=kLoop, calls=%fused_computation.19 | loop fusion | flops 14667776 | bytes 8466432 | tf_op jit(solution)/shard_map/reduce_sum | solution.py:55
  176.9 25.4 %all-gather = f32[8192]{0:T(1024)S(1)} all-gather(f32[1024]{0:T(1024)S(1)} %add_add_fusion), channel_id=2, replica_groups=mesh['req'=64,'voc'=8] {'voc'}, dimensions={0}, use_global_device_ids=true | all-gather | bytes 36864 | tf_op jit(solution)/shard_map/all_gather | solution.py:8
  202.3 0.1 add_bitcast_fusion
  202.4 24.5 %all-gather.2 = f32[8,1,1024]{2,1,0:T(1,128)S(1)} all-gather(f32[1,1,1024]{2,1,0:T(1,128)S(1)} %get-tuple-element.94), channel_id=1, replica_groups=mesh['req'=64,'voc'=8] {'voc'}, dimensions={0}, use_global_device_ids=true | all-gather | bytes 36864 | tf_op jit(solution)/shard_map/all_gather | solution.py:8
  226.9 24.5 %all-gather.1 = f32[8,1,1024]{2,1,0:T(1,128)S(1)} all-gather(f32[1,1,1024]{2,1,0:T(1,128)S(1)} %get-tuple-element.95), channel_id=1, replica_groups=mesh['req'=64,'voc'=8] {'voc'}, dimensions={0}, use_global_device_ids=true | all-gather | bytes 36864 | tf_op jit(solution)/shard_map/all_gather | solution.py:8
  251.3 24.5 %all-gather.3 = f32[8,1,1024]{2,1,0:T(1,128)S(1)} all-gather(f32[1,1,1024]{2,1,0:T(1,128)S(1)} %get-tuple-element.88), channel_id=1, replica_groups=mesh['req'=64,'voc'=8] {'voc'}, dimensions={0}, use_global_device_ids=true | all-gather | bytes 36864 | tf_op jit(solution)/shard_map/all_gather | solution.py:8
  275.8 0.8 while.16
  276.7 0.0 copy-done.1
  276.7 0.6 subtract_multiply_fusion
  (59 shorter events, 0.5 us)
Async XLA Ops:
  7.2 155.2 %copy-start.3 = (f32[1600]{0:T(1024)S(1)}, f32[1600]{0:T(1024)}, u32[]{:S(2)}) copy-start(f32[1600]{0:T(1024)} %param.8) | copy-start | bytes 19204
  7.2 64.9 %all-gather.8.cloned.1.call-start = ((), (), s32[]{:S(2)}) async-start(), calls=%async_computation | async-start | bytes 3686400 | tf_op jit(solution)/shard_map/all_gather | solution.py:28
  7.9 154.4 %all-gather.10.cloned.1.call-start = ((), (), s32[]{:S(2)}) async-start(), calls=%async_computation.1 | async-start | bytes 6922240 | tf_op jit(solution)/shard_map/all_gather | solution.py:41
  72.1 90.2 %copy-start = (bf16[1024,1600]{0,1:T(8,128)(2,1)S(1)}, bf16[1024,1600]{0,1:T(8,128)(2,1)}, u32[]{:S(2)}) copy-start(bf16[1024,1600]{0,1:T(8,128)(2,1)} %all-gather.8.cloned.1.call-done) | copy-start | bytes 9830404
  162.3 3.8 %copy-start.2 = (bf16[2048,1600]{1,0:T(8,128)(2,1)S(1)}, bf16[2048,1600]{1,0:T(8,128)(2,1)}, u32[]{:S(2)}) copy-start(bf16[2048,1600]{1,0:T(8,128)(2,1)} %all-gather.10.cloned.1.call-done) | copy-start | bytes 19660804
  172.9 103.7 %copy-start.1 = (s32[128]{0:T(128)S(1)}, s32[128]{0:T(128)}, u32[]{:S(2)}) copy-start(s32[128]{0:T(128)} %param.11) | copy-start | bytes 1540
Sparse Core Ops, SparseCore 0:
  10.0 62.0 all-gather.7
  75.4 86.8 all-gather.9
where the time goes:
time: 284 us
  waiting for transfers between devices  136 us (48%)
  blocking collectives  115 us (40%)
  between operations  14.2 us (5%)
  matrix products  10.6 us (4%)
  other arithmetic  7.67 us (3%)
    all_gather x4, blocking collectives, merged_2(): pieces = jax.tree.map(lambda part: lax.all_gather(part, axis), value)  98.8 us
    all_gather x1, waiting for transfers between devices, on_device(): whole = lax.all_gather(unembed, 'req', axis=0, tiled=True)  87.4 us
    all_gather x1, waiting for transfers between devices, on_device(): lax.all_gather(hidden, 'voc', axis=0, tiled=True)  46.9 us
    all_gather x1, blocking collectives, on_device(): lax.all_gather(targets, 'voc', axis=0, tiled=True)  16.5 us
    dot_general x4, matrix products, on_device(): lax.dot_general(normed, piece, (((1,), (1,)), ((), ())), preferred_elemen...  10.6 us
  transfers between devices with their start and end apart: 2, of which 2 were waited for; matrix products, arithmetic and copies ran while one was open for 1% of the time, Pallas kernels for 0%

commit v1 on v0

--- a/solution.py
+++ b/solution.py
@@ -2,6 +2,27 @@
 import jax.numpy as jnp
 from jax import lax
 from jax.sharding import PartitionSpec as P
+
+
+def ring_gather(x, axis, dim):
+    count, here, width = (lax.axis_size(axis), lax.axis_index(axis), x.shape[dim])
+    right = [(i, (i + 1) % count) for i in range(count)]
+    left = [(i, (i - 1) % count) for i in range(count)]
+    out = jnp.zeros((*x.shape[:dim], count * width, *x.shape[dim + 1 :]), x.dtype)
+    out = lax.dynamic_update_slice_in_dim(out, x, here * width, axis=dim)
+    from_left = from_right = x
+    middle = count // 2
+    for turn in range(1, middle + 1):
+        from_left = lax.ppermute(from_left, axis, right)
+        out = lax.dynamic_update_slice_in_dim(
+            out, from_left, (here - turn) % count * width, axis=dim
+        )
+        if turn < count - middle:
+            from_right = lax.ppermute(from_right, axis, left)
+            out = lax.dynamic_update_slice_in_dim(
+                out, from_right, (here + turn) % count * width, axis=dim
+            )
+    return out
 
 
 def merged_2(value, axis, join):
@@ -25,7 +46,7 @@
 
 def on_device(hidden, norm_gain, unembed, targets, live):
     rows, wanted = (
-        lax.all_gather(hidden, "voc", axis=0, tiled=True),
+        ring_gather(hidden, "voc", 0),
         lax.all_gather(targets, "voc", axis=0, tiled=True),
     )
     wide = rows.astype(jnp.float32)

time: 284 us -> 226 us (0.80)
  waiting for transfers between devices: 136 us -> 49.6 us
  starting transfers between devices: 0.08 us -> 20.6 us
  blocking collectives: 115 us -> 120 us
  local copies, waits for them, and re-layouts: 0.27 us -> 3.8 us
    all_gather x1, waiting for transfers between devices: 87.4 us -> 31.7 us  [on_device(): whole = lax.all_gather(unembed, 'req', axis=0, tiled=True)]
    all_gather x1 -> x0, waiting for transfers between devices: 46.9 us -> none  [on_device(): lax.all_gather(hidden, 'voc', axis=0, tiled=True)]
    ppermute x0 -> x7, starting transfers between devices: none -> 20.6 us  [the longest x4 12.8 us: ring_gather(): from_left = lax.ppermute(from_left, axis, right)]
    ppermute x0 -> x7, waiting for transfers between devices: none -> 17.3 us  [the longest x4 16.8 us: ring_gather(): from_left = lax.ppermute(from_left, axis, right)]
    all_gather x1, blocking collectives: 16.5 us -> 21.3 us  [on_device(): lax.all_gather(targets, 'voc', axis=0, tiled=True)]
    dynamic_update_slice x0 -> x8, local copies, waits for them, and re-layouts: none -> 3.12 us  [the longest x4 1.56 us: ring_gather(): lax.dynamic_update_slice_in_dim(out, from_left, (here - turn) % count * w...]
  transfers between devices with their start and end apart: 2 -> 8, of which waited for: 2 -> 6; matrix products, arithmetic and copies ran while one was open for 1% -> 2% of each run, Pallas kernels for 0% -> 0%
where the time goes in v1:
time: 226 us; the launch traced here: 225 us
  blocking collectives  120 us (53%)
  waiting for transfers between devices  49.6 us (22%)
  starting transfers between devices  20.6 us (9%)
  between operations  14.5 us (6%)
  matrix products  10.6 us (5%)
  other arithmetic  5.59 us (2%)
  local copies, waits for them, and re-layouts  3.8 us (2%)
    all_gather x4, blocking collectives, merged_2(): pieces = jax.tree.map(lambda part: lax.all_gather(part, axis), value)  98.8 us
    all_gather x1, waiting for transfers between devices, on_device(): whole = lax.all_gather(unembed, 'req', axis=0, tiled=True)  31.7 us
    all_gather x1, blocking collectives, on_device(): lax.all_gather(targets, 'voc', axis=0, tiled=True)  21.3 us
    ppermute x4, waiting for transfers between devices, ring_gather(): from_left = lax.ppermute(from_left, axis, right)  16.8 us
    ppermute x4, starting transfers between devices, ring_gather(): from_left = lax.ppermute(from_left, axis, right)  12.8 us
    dot_general x4, matrix products, on_device(): lax.dot_general(normed, piece, (((1,), (1,)), ((), ())), preferred_elemen...  10.6 us
    ppermute x3, starting transfers between devices, ring_gather(): from_right = lax.ppermute(from_right, axis, left)  7.76 us
  transfers between devices with their start and end apart: 8, of which 6 were waited for; matrix products, arithmetic and copies ran while one was open for 2% of the time, Pallas kernels for 0%

profile of v1, /device:TPU:16, one launch (start us, length us, event | category | flops | bytes accessed | tf_op | source)
XLA Modules:
  0.0 225.2 jit_solution(15369719771815912018)
XLA Ops:
  7.2 0.0 all-gather.7.cloned.1.call-start
  7.2 0.7 all-gather.7.cloned.1.call-update
  7.9 3.5 %collective-permute-start = (bf16[128,1600]{0,1:T(8,128)(2,1)}, bf16[128,1600]{0,1:T(8,128)(2,1)}, u32[]{:S(2)}, u32[]{:S(2)}) collective-permute-start(bf16[128,1600]{0,1:T(8,128)(2,1)} %param.7), channel_id=1, source_target_pairs={{0,1},{1,2},{2,3},{3,4},{4,5},{5,6},{6,7},{7,0},{8,9},{9,10},{10,1... | collective-permute-start | bytes 1228808 | tf_op jit(solution)/shard_map/ppermute | solution.py:16
  11.4 2.4 %collective-permute-start.1 = (bf16[128,1600]{0,1:T(8,128)(2,1)}, bf16[128,1600]{0,1:T(8,128)(2,1)}, u32[]{:S(2)}, u32[]{:S(2)}) collective-permute-start(bf16[128,1600]{0,1:T(8,128)(2,1)} %param.7), channel_id=1, source_target_pairs={{0,7},{1,0},{2,1},{3,2},{4,3},{5,4},{6,5},{7,6},{8,15},{9,8},{10,9... | collective-permute-start | bytes 1228808 | tf_op jit(solution)/shard_map/ppermute | solution.py:21
  13.9 0.0 copy-start
  13.9 21.3 %all-gather.4 = s32[8,1,128]{2,1,0:T(1,128)S(1)} all-gather(s32[1,1,128]{2,1,0:T(1,128)} %bitcast.74), channel_id=1, replica_groups=mesh['req'=64,'voc'=8] {'voc'}, dimensions={0}, use_global_device_ids=true | all-gather | bytes 4608 | tf_op jit(solution)/shard_map/all_gather | solution.py:50
  35.3 0.4 broadcast_in_dim.13
  35.7 0.0 copy-done
  35.7 0.1 constant_dynamic-update-slice_fusion.7
  35.8 0.0 collective-permute-done
  35.8 2.8 %collective-permute-start.2 = (bf16[128,1600]{0,1:T(8,128)(2,1)}, bf16[128,1600]{0,1:T(8,128)(2,1)S(1)}, u32[]{:S(2)}, u32[]{:S(2)}) collective-permute-start(bf16[128,1600]{0,1:T(8,128)(2,1)} %collective-permute-done), channel_id=1, source_target_pairs={{0,1},{1,2},{2,3},{3,4},{4,5},{5,6},{6,7},{7,0},{8,9},{9,10},{10,1... | collective-permute-start | bytes 1228808 | tf_op jit(solution)/shard_map/ppermute | solution.py:16
  38.6 0.0 collective-permute-done.1
  38.6 3.1 %collective-permute-start.3 = (bf16[128,1600]{0,1:T(8,128)(2,1)}, bf16[128,1600]{0,1:T(8,128)(2,1)S(1)}, u32[]{:S(2)}, u32[]{:S(2)}) collective-permute-start(bf16[128,1600]{0,1:T(8,128)(2,1)} %collective-permute-done.1), channel_id=1, source_target_pairs={{0,7},{1,0},{2,1},{3,2},{4,3},{5,4},{6,5},{7,6},{8,15},{9,8},{10,9... | collective-permute-start | bytes 1228808 | tf_op jit(solution)/shard_map/ppermute | solution.py:21
  41.7 1.1 constant_dynamic-update-slice_fusion.6
  42.9 1.1 constant_dynamic-update-slice_fusion.5
  44.0 2.2 collective-permute-done.2
  46.2 3.5 %collective-permute-start.4 = (bf16[128,1600]{0,1:T(8,128)(2,1)S(1)}, bf16[128,1600]{0,1:T(8,128)(2,1)S(1)}, u32[]{:S(2)}, u32[]{:S(2)}) collective-permute-start(bf16[128,1600]{0,1:T(8,128)(2,1)S(1)} %collective-permute-done.2), channel_id=1, source_target_pairs={{0,1},{1,2},{2,3},{3,4},{4,5},{5,6},{6,7},{7,0},{8,9},{9,10},{10,1... | collective-permute-start | bytes 1228808 | tf_op jit(solution)/shard_map/ppermute | solution.py:16
  49.7 0.4 collective-permute-done.3
  50.1 2.3 %collective-permute-start.5 = (bf16[128,1600]{0,1:T(8,128)(2,1)S(1)}, bf16[128,1600]{0,1:T(8,128)(2,1)S(1)}, u32[]{:S(2)}, u32[]{:S(2)}) collective-permute-start(bf16[128,1600]{0,1:T(8,128)(2,1)S(1)} %collective-permute-done.3), channel_id=1, source_target_pairs={{0,7},{1,0},{2,1},{3,2},{4,3},{5,4},{6,5},{7,6},{8,15},{9,8},{10,9... | collective-permute-start | bytes 1228808 | tf_op jit(solution)/shard_map/ppermute | solution.py:21
  52.4 0.1 constant_dynamic-update-slice_fusion.4
  52.6 0.0 copy-start.3
  52.6 0.1 constant_dynamic-update-slice_fusion.3
  52.8 5.0 %collective-permute-done.4 = bf16[128,1600]{0,1:T(8,128)(2,1)S(1)} collective-permute-done((bf16[128,1600]{0,1:T(8,128)(2,1)S(1)}, bf16[128,1600]{0,1:T(8,128)(2,1)S(1)}, u32[]{:S(2)}, u32[]{:S(2)}) %collective-permute-start.4) | collective-permute-done | bytes 409632 | tf_op jit(solution)/shard_map/ppermute | solution.py:16
  57.8 3.1 %collective-permute-start.6 = (bf16[128,1600]{0,1:T(8,128)(2,1)S(1)}, bf16[128,1600]{0,1:T(8,128)(2,1)S(1)}, u32[]{:S(2)}, u32[]{:S(2)}) collective-permute-start(bf16[128,1600]{0,1:T(8,128)(2,1)S(1)} %collective-permute-done.4), channel_id=1, source_target_pairs={{0,1},{1,2},{2,3},{3,4},{4,5},{5,6},{6,7},{7,0},{8,9},{9,10},{10,1... | collective-permute-start | bytes 1228808 | tf_op jit(solution)/shard_map/ppermute | solution.py:16
  60.9 0.1 constant_dynamic-update-slice_fusion.2
  61.0 0.1 collective-permute-done.5
  61.2 0.1 constant_dynamic-update-slice_fusion.1
  61.3 9.5 %collective-permute-done.6 = bf16[128,1600]{0,1:T(8,128)(2,1)S(1)} collective-permute-done((bf16[128,1600]{0,1:T(8,128)(2,1)S(1)}, bf16[128,1600]{0,1:T(8,128)(2,1)S(1)}, u32[]{:S(2)}, u32[]{:S(2)}) %collective-permute-start.6) | collective-permute-done | bytes 409632 | tf_op jit(solution)/shard_map/ppermute | solution.py:16
  70.8 0.1 constant_dynamic-update-slice_fusion
  71.0 0.8 fusion
  71.7 31.7 %all-gather.7.cloned.1.call-done = bf16[2048,1600]{1,0:T(8,128)(2,1)} async-done(((bf16[32,1600]{1,0:T(8,128)(2,1)}), bf16[2048,1600]{1,0:T(8,128)(2,1)}) %all-gather.7.cloned.1.call-update) | async-done | bytes 6553616 | tf_op jit(solution)/shard_map/all_gather | solution.py:62
  103.4 0.0 copy-done.3
  103.4 0.0 copy-start.2
  103.4 3.8 %fusion.47 = (f32[1024]{0:T(1024)S(1)}, f32[1024,512]{0,1:T(8,128)S(1)}) fusion(bf16[1024,1600]{0,1:T(8,128)(2,1)S(1)} %constant_dynamic-update-slice_fusion, f32[1600]{0:T(1024)S(1)} %copy-done.3, f32[1024]{0:T(1024)S(1)} %add_rsqrt_fusion, bf16[2048,1600]{1,0:T(8,128)(2,1)} %all-gather.7.cloned.1.call-done), kind=kOutput, calls=%fused_computation.114 | convolution fusion | flops 1684798464 | bytes 7092480 | tf_op jit(solution)/shard_map/dot_general | solution.py:67
  107.2 0.0 copy-done.2
  107.2 2.2 fusion.46
  109.5 2.2 fusion.45
  111.7 2.2 fusion.44
  114.0 0.0 copy-start.1
  114.0 3.9 %fusion.3 = (f32[1024]{0:T(1024)S(1)}, f32[1024]{0:T(1024)S(1)}, f32[1024]{0:T(1024)S(1)}, f32[1024]{0:T(1024)S(1)}, f32[1024]{0:T(1024)S(1)}, /*index=5*/f32[10...) fusion(f32[1024,512]{0,1:T(8,128)S(1)} %get-tuple-element.108, ...), kind=kLoop, calls=%fused_computation.19 | loop fusion | flops 14667776 | bytes 8466432 | tf_op jit(solution)/shard_map/reduce_sum | solution.py:76
  117.9 25.4 %all-gather = f32[8192]{0:T(1024)S(1)} all-gather(f32[1024]{0:T(1024)S(1)} %add_add_fusion), channel_id=2, replica_groups=mesh['req'=64,'voc'=8] {'voc'}, dimensions={0}, use_global_device_ids=true | all-gather | bytes 36864 | tf_op jit(solution)/shard_map/all_gather | solution.py:29
  143.3 0.1 add_bitcast_fusion
  143.4 24.5 %all-gather.2 = f32[8,1,1024]{2,1,0:T(1,128)S(1)} all-gather(f32[1,1,1024]{2,1,0:T(1,128)S(1)} %get-tuple-element.94), channel_id=1, replica_groups=mesh['req'=64,'voc'=8] {'voc'}, dimensions={0}, use_global_device_ids=true | all-gather | bytes 36864 | tf_op jit(solution)/shard_map/all_gather | solution.py:29
  167.9 24.5 %all-gather.1 = f32[8,1,1024]{2,1,0:T(1,128)S(1)} all-gather(f32[1,1,1024]{2,1,0:T(1,128)S(1)} %get-tuple-element.95), channel_id=1, replica_groups=mesh['req'=64,'voc'=8] {'voc'}, dimensions={0}, use_global_device_ids=true | all-gather | bytes 36864 | tf_op jit(solution)/shard_map/all_gather | solution.py:29
  192.4 24.5 %all-gather.3 = f32[8,1,1024]{2,1,0:T(1,128)S(1)} all-gather(f32[1,1,1024]{2,1,0:T(1,128)S(1)} %get-tuple-element.88), channel_id=1, replica_groups=mesh['req'=64,'voc'=8] {'voc'}, dimensions={0}, use_global_device_ids=true | all-gather | bytes 36864 | tf_op jit(solution)/shard_map/all_gather | solution.py:29
  216.9 0.8 while.16
  217.7 0.0 copy-done.1
  217.7 0.6 subtract_multiply_fusion
  (59 shorter events, 0.5 us)
Async XLA Ops:
  7.2 96.2 %all-gather.7.cloned.1.call-start = ((), (), s32[]{:S(2)}) async-start(), calls=%async_computation | async-start | bytes 6922240 | tf_op jit(solution)/shard_map/all_gather | solution.py:62
  7.9 27.9 %collective-permute-start = (bf16[128,1600]{0,1:T(8,128)(2,1)}, bf16[128,1600]{0,1:T(8,128)(2,1)}, u32[]{:S(2)}, u32[]{:S(2)}) collective-permute-start(bf16[128,1600]{0,1:T(8,128)(2,1)} %param.7), channel_id=1, source_target_pairs={{0,1},{1,2},{2,3},{3,4},{4,5},{5,6},{6,7},{7,0},{8,9},{9,10},{10,1... | collective-permute-start | bytes 1228808 | tf_op jit(solution)/shard_map/ppermute | solution.py:16
  11.4 27.2 %collective-permute-start.1 = (bf16[128,1600]{0,1:T(8,128)(2,1)}, bf16[128,1600]{0,1:T(8,128)(2,1)}, u32[]{:S(2)}, u32[]{:S(2)}) collective-permute-start(bf16[128,1600]{0,1:T(8,128)(2,1)} %param.7), channel_id=1, source_target_pairs={{0,7},{1,0},{2,1},{3,2},{4,3},{5,4},{6,5},{7,6},{8,15},{9,8},{10,9... | collective-permute-start | bytes 1228808 | tf_op jit(solution)/shard_map/ppermute | solution.py:21
  13.9 21.8 %copy-start = (bf16[128,1600]{0,1:T(8,128)(2,1)S(1)}, bf16[128,1600]{0,1:T(8,128)(2,1)}, u32[]{:S(2)}) copy-start(bf16[128,1600]{0,1:T(8,128)(2,1)} %param.7) | copy-start | bytes 1228804
  35.8 10.4 %collective-permute-start.2 = (bf16[128,1600]{0,1:T(8,128)(2,1)}, bf16[128,1600]{0,1:T(8,128)(2,1)S(1)}, u32[]{:S(2)}, u32[]{:S(2)}) collective-permute-start(bf16[128,1600]{0,1:T(8,128)(2,1)} %collective-permute-done), channel_id=1, source_target_pairs={{0,1},{1,2},{2,3},{3,4},{4,5},{5,6},{6,7},{7,0},{8,9},{9,10},{10,1... | collective-permute-start | bytes 1228808 | tf_op jit(solution)/shard_map/ppermute | solution.py:16
  38.6 11.5 %collective-permute-start.3 = (bf16[128,1600]{0,1:T(8,128)(2,1)}, bf16[128,1600]{0,1:T(8,128)(2,1)S(1)}, u32[]{:S(2)}, u32[]{:S(2)}) collective-permute-start(bf16[128,1600]{0,1:T(8,128)(2,1)} %collective-permute-done.1), channel_id=1, source_target_pairs={{0,7},{1,0},{2,1},{3,2},{4,3},{5,4},{6,5},{7,6},{8,15},{9,8},{10,9... | collective-permute-start | bytes 1228808 | tf_op jit(solution)/shard_map/ppermute | solution.py:21
  46.2 11.6 %collective-permute-start.4 = (bf16[128,1600]{0,1:T(8,128)(2,1)S(1)}, bf16[128,1600]{0,1:T(8,128)(2,1)S(1)}, u32[]{:S(2)}, u32[]{:S(2)}) collective-permute-start(bf16[128,1600]{0,1:T(8,128)(2,1)S(1)} %collective-permute-done.2), channel_id=1, source_target_pairs={{0,1},{1,2},{2,3},{3,4},{4,5},{5,6},{6,7},{7,0},{8,9},{9,10},{10,1... | collective-permute-start | bytes 1228808 | tf_op jit(solution)/shard_map/ppermute | solution.py:16
  50.1 11.0 %collective-permute-start.5 = (bf16[128,1600]{0,1:T(8,128)(2,1)S(1)}, bf16[128,1600]{0,1:T(8,128)(2,1)S(1)}, u32[]{:S(2)}, u32[]{:S(2)}) collective-permute-start(bf16[128,1600]{0,1:T(8,128)(2,1)S(1)} %collective-permute-done.3), channel_id=1, source_target_pairs={{0,7},{1,0},{2,1},{3,2},{4,3},{5,4},{6,5},{7,6},{8,15},{9,8},{10,9... | collective-permute-start | bytes 1228808 | tf_op jit(solution)/shard_map/ppermute | solution.py:21
  52.6 50.8 %copy-start.3 = (f32[1600]{0:T(1024)S(1)}, f32[1600]{0:T(1024)}, u32[]{:S(2)}) copy-start(f32[1600]{0:T(1024)} %param.8) | copy-start | bytes 19204
  57.8 13.0 %collective-permute-start.6 = (bf16[128,1600]{0,1:T(8,128)(2,1)S(1)}, bf16[128,1600]{0,1:T(8,128)(2,1)S(1)}, u32[]{:S(2)}, u32[]{:S(2)}) collective-permute-start(bf16[128,1600]{0,1:T(8,128)(2,1)S(1)} %collective-permute-done.4), channel_id=1, source_target_pairs={{0,1},{1,2},{2,3},{3,4},{4,5},{5,6},{6,7},{7,0},{8,9},{9,10},{10,1... | collective-permute-start | bytes 1228808 | tf_op jit(solution)/shard_map/ppermute | solution.py:16
  103.4 3.8 %copy-start.2 = (bf16[2048,1600]{1,0:T(8,128)(2,1)S(1)}, bf16[2048,1600]{1,0:T(8,128)(2,1)}, u32[]{:S(2)}) copy-start(bf16[2048,1600]{1,0:T(8,128)(2,1)} %all-gather.7.cloned.1.call-done) | copy-start | bytes 19660804
  114.0 103.7 %copy-start.1 = (s32[128]{0:T(128)S(1)}, s32[128]{0:T(128)}, u32[]{:S(2)}) copy-start(s32[128]{0:T(128)} %param.11) | copy-start | bytes 1540
Sparse Core Ops, SparseCore 0:
  11.3 92.0 all-gather.6
